TPU v7x, 32 devices: a whole 2x2x4 slice. The times are simulated.
32 devices in a mesh: tile: 8 (over y, x, core), dir: 4 (over z).
Axes of the slice: x: 2, y: 2, z: 4, core: 2. Of those that a mesh axis runs over, the one named last changes fastest.
Arguments:
- screens: bfloat16 [6, 512, 2048], P(None, 'tile'), may hold values from -13 to 13
- ray_shift: int32 [16, 6, 2], P('dir'), may hold values from -128 to 2047, as said below
- ray_weight: float32 [16, 6, 4], P('dir'), may hold values from 0 to 0.5
- influence_index: int32 [512, 16, 16], P('tile', 'dir'), may hold values from 0 to 69, as said below
- influence: bfloat16 [512, 16, 16, 128], P('tile', 'dir'), may hold values from 0 to 0.22
- pupil_mask: int32 [512, 2048], P('tile', 'dir'), may hold values 0 or 1
- petal: int32 [24, 48], P('tile', 'dir'), may hold values from 0 to 6
Outputs:
- commands: float32 [24, 48], P('tile', 'dir')
- corrected: bfloat16 [16, 512, 2048], P('dir', 'tile')
Inputs may be any that keep to these rules, and one draw needn't show every extreme that they name: ray_shift[..., 0], the row offset, lies in -128 to 127 and reaches both ends; ray_shift[..., 1], the column offset, lies in 0 to 2047. `influence_index`: each entry names a grid point of the tile's own actuator block extended by one actuator on each side, flattened row by row with 14 points a row; entries may repeat.
All inputs are finite; a program needn't handle non-finite values. No bound on the sum of `pupil_mask` on one device may be relied on, other than what follows from the above.
Results may differ from a plain program's by a relative error of at most 0.007.
Values may be sent and summed in bfloat16 or wider, within the bound.
No kernel may reach another device: no remote copies, remote signals or barrier semaphores. Data moves between devices by JAX's collectives and lax.ppermute only.
A program may use at most 128 MiB of HBM per device.

v0:
```python
import jax
import jax.numpy as jnp
from jax import lax
from jax.sharding import PartitionSpec as P

SPAN = 2
AR_DEV = 3
AC_DEV = 12
ITERS = 3
ridge_weight = 1.0
piston_weight = 0.002
highest = lax.Precision.HIGHEST


def passed_along(array, axis, by):
    size = lax.axis_size(axis)
    return lax.ppermute(array, axis, [(i, (i + by) % size) for i in range(size)])


def padded_2(array, sides, width):
    for axis, dim in sides:
        size, length = (lax.axis_size(axis), array.shape[dim])
        up = [(i, (i + 1) % size) for i in range(size - 1)]
        down = [(j, i) for i, j in up]
        last = lax.slice_in_dim(array, length - width, length, axis=dim)
        first = lax.slice_in_dim(array, 0, width, axis=dim)
        before = lax.ppermute(last, axis, up)
        after = lax.ppermute(first, axis, down)
        array = jnp.concatenate([before, array, after], axis=dim)
    return array


def band_stack_whole(piece):
    bands = []
    for offset in range(SPAN, -SPAN - 1, -1):
        if offset == 0:
            bands.append(piece)
        else:
            bands.append(passed_along(piece, "tile", offset))
    return jnp.concatenate(bands, axis=1)


def trace_rows(padded_rim, shifts, layer_gains, rim_depth, band_rows):
    summed = jnp.zeros((band_rows, padded_rim.shape[2]), jnp.float32)
    for layer_index in range(padded_rim.shape[0]):
        window = lax.dynamic_slice_in_dim(
            padded_rim[layer_index], rim_depth + shifts[layer_index, 0], band_rows + 1, 0
        ).astype(jnp.float32)
        window = jnp.roll(window, -shifts[layer_index, 1], axis=1)
        beside = jnp.roll(window, -1, axis=1)
        gains = layer_gains[layer_index]
        summed = summed + (
            gains[0] * window[:-1]
            + gains[1] * beside[:-1]
            + gains[2] * window[1:]
            + gains[3] * beside[1:]
        )
    return summed


def fold_rims(gathered):
    padded = padded_2(gathered, (("tile", 0), ("dir", 1)), 1)
    grid_rows = gathered.shape[0] - 2
    grid_columns = gathered.shape[1] - 2
    interior = gathered[1:-1, 1:-1]
    interior = interior.at[:, 0].add(padded[2 : grid_rows + 2, 0])
    interior = interior.at[:, -1].add(padded[2 : grid_rows + 2, -1])
    interior = interior.at[0, :].add(padded[0, 2 : grid_columns + 2])
    interior = interior.at[-1, :].add(padded[-1, 2 : grid_columns + 2])
    interior = interior.at[0, 0].add(padded[0, 0])
    interior = interior.at[0, -1].add(padded[0, -1])
    interior = interior.at[-1, 0].add(padded[-1, 0])
    interior = interior.at[-1, -1].add(padded[-1, -1])
    return interior


def on_device(screens, ray_shift, ray_weight, influence_index, influence, pupil_mask, petal):
    band_rows = screens.shape[1]
    rim_depth = SPAN * band_rows
    padded_rim = band_stack_whole(screens)
    phases = [
        trace_rows(padded_rim, ray_shift[member], ray_weight[member], rim_depth, band_rows)
        for member in range(ray_shift.shape[0])
    ]
    direction_count = ray_shift.shape[0] * lax.axis_size("dir")
    summed = phases[0]
    for member in range(1, len(phases)):
        summed = summed + phases[member]
    mean_phase = (
        lax.psum_scatter(
            summed.astype(jnp.bfloat16), "dir", scatter_dimension=1, tiled=True
        ).astype(jnp.float32)
        / direction_count
    )
    tiles_here = influence.shape[1]
    near_count = influence.shape[2]
    values = influence.astype(jnp.float32)
    extent = (AR_DEV + 2) * (AC_DEV + 2)
    selector = (
        influence_index.reshape(-1)[:, None] == jnp.arange(extent, dtype=jnp.int32)[None, :]
    ).astype(jnp.float32)
    weights = pupil_mask.astype(jnp.float32)
    active = (petal < 6).astype(jnp.float32)
    petals = (petal.reshape(-1)[:, None] == jnp.arange(6, dtype=jnp.int32)[None, :]).astype(
        jnp.float32
    )

    def surface(commands):
        extended = padded_2(commands, (("tile", 0), ("dir", 1)), 1)
        picked = jnp.dot(selector, extended.reshape(-1), precision=highest).reshape(
            band_rows, tiles_here, near_count
        )
        tile_sums = jnp.einsum("rckp,rck->rcp", values, picked, precision=highest)
        return tile_sums.reshape(band_rows, tiles_here * 128)

    def spread(field):
        tile_terms = jnp.einsum(
            "rckp,rcp->rck", values, field.reshape(band_rows, tiles_here, 128), precision=highest
        )
        gathered = jnp.dot(tile_terms.reshape(-1), selector, precision=highest).reshape(
            AR_DEV + 2, AC_DEV + 2
        )
        return fold_rims(gathered)

    def global_norm(residual):
        return lax.psum(jnp.sum(residual * residual), ("tile", "dir"))

    rhs = active * spread(weights * mean_phase)
    commands = jnp.zeros_like(rhs)
    residual = rhs
    direction = rhs
    norm_now = global_norm(residual)
    for step_index in range(ITERS):
        local_part = active * spread(weights * surface(direction)) + ridge_weight * direction
        local_totals = jnp.dot(direction.reshape(-1), petals, precision=highest)
        petal_totals, partial_dot = lax.psum(
            (local_totals, jnp.sum(direction * local_part)), ("tile", "dir")
        )
        applied = local_part + piston_weight * jnp.dot(
            petals, petal_totals, precision=highest
        ).reshape(direction.shape)
        curvature = partial_dot + piston_weight * jnp.sum(petal_totals * petal_totals)
        step_size = norm_now / curvature
        commands = commands + step_size * direction
        residual = residual - step_size * applied
        norm_next = global_norm(residual)
        direction = residual + norm_next / norm_now * direction
        norm_now = norm_next
    fitted = surface(commands)
    whole_band = lax.all_gather(fitted.astype(jnp.bfloat16), "dir", axis=1, tiled=True).astype(
        fitted.dtype
    )
    corrected = jnp.stack([(phase_rows - whole_band).astype(jnp.bfloat16) for phase_rows in phases])
    return (commands, corrected)


def solution(mesh):
    in_specs = (
        P(None, "tile", None),
        P("dir", None, None),
        P("dir", None, None),
        P("tile", "dir", None),
        P("tile", "dir", None, None),
        P("tile", "dir"),
        P("tile", "dir"),
    )
    out_specs = (P("tile", "dir"), P("dir", "tile", None))
    return jax.shard_map(
        on_device, mesh=mesh, in_specs=in_specs, out_specs=out_specs, check_vma=False
    )
```

profile of v0, /device:TPU:4, one launch (start us, length us, event | category | flops | bytes accessed | tf_op | source)
XLA Modules:
  0.0 727.7 jit_solution(10193905271201965904)
XLA Ops:
  70.6 6.6 collective-permute-done.1
  80.4 30.4 %collective-permute-done.3 = bf16[6,64,2048]{2,1,0:T(8,128)(2,1)S(1)} collective-permute-done((bf16[6,64,2048]{2,1,0:T(8,128)(2,1)}, bf16[6,64,2048]{2,1,0:T(8,128)(2,1)S(1)}, u32[]{:S(2)}, u32[]{:S(2)}) %collective-permute-start.3) | collective-permute-done | bytes 1572896 | tf_op jit(solution)/shard_map/ppermute | solution.py:17
  162.1 96.7 %add_convert_fusion = (bf16[64,2048]{1,0:T(8,128)(2,1)}, f32[64,2048]{1,0:T(8,128)}, f32[64,2048]{1,0:T(8,128)}, f32[64,2048]{1,0:T(8,128)}, f32[64,2048]{1,0:T(8,128)}) fusion(f32[65,1]{1,0:T(8,128)} %slice.2466, f32[65,2047]{1,0:T(8,128)} %slice.2465, f32[]{:T(128)} %bitcast.97, f32[65,2048]{1,0:T(8,128)} %copy-done.28, f32[]{:T(128)} %bitcast.96, ...), kind=kLoop, calls=%fused_computation.395 | loop fusion | flops 31457280 | bytes 40305024 | tf_op jit(solution)/shard_map/convert_element_type | solution.py:91
  262.5 17.6 %reduce-scatter.2.cloned.1.call-done = bf16[64,512]{1,0:T(8,128)(2,1)} async-done(((bf16[64,2048]{1,0:T(8,128)(2,1)}), bf16[64,512]{1,0:T(8,128)(2,1)}) %reduce-scatter.2.cloned.1.call-update) | async-done | bytes 65552 | tf_op jit(solution)/shard_map/reduce_scatter | solution.py:90
  286.2 4.5 collective-permute-start.5
  314.0 4.5 collective-permute-start.9
  319.9 3.7 collective-permute-start.10
  324.9 4.2 collective-permute-done.11
  338.0 4.5 collective-permute-start.13
  365.5 38.8 %all-reduce.2 = (f32[6]{0:T(128)S(1)}, f32[]{:T(128)}, f32[]{:T(128)}) all-reduce(f32[6]{0:T(128)S(1)} %convolution_bitcast_fusion.4, f32[]{:T(128)} %get-tuple-element.388, f32[]{:T(128)} %get-tuple-element.387), channel_id=1, replica_groups=mesh['tile'=8,'dir'=4] {'tile','dir'}, use_global_device_ids=true, to_apply=%region_7.9 | all-reduce | flops 8 | bytes 64 | tf_op jit(solution)/shard_map/psum | solution.py:136
  407.9 42.2 %psum.66 = f32[]{:T(128)} all-reduce(f32[]{:T(128)} %get-tuple-element.398), channel_id=1, replica_groups=mesh['tile'=8,'dir'=4] {'tile','dir'}, use_global_device_ids=true, to_apply=%region_10.12 | all-reduce | flops 1 | bytes 8 | tf_op jit(solution)/shard_map/psum | solution.py:126
  453.5 4.5 collective-permute-start.17
  462.7 4.2 collective-permute-done.19
  475.7 4.5 collective-permute-start.21
  503.2 40.5 %all-reduce.1 = (f32[6]{0:T(128)S(1)}, f32[]{:T(128)}) all-reduce(f32[6]{0:T(128)S(1)} %convolution_bitcast_fusion.2, f32[]{:T(128)} %multiply_reduce_fusion.1), channel_id=1, replica_groups=mesh['tile'=8,'dir'=4] {'tile','dir'}, use_global_device_ids=true, to_apply=%region_13.15 | all-reduce | flops 7 | bytes 56 | tf_op jit(solution)/shard_map/psum | solution.py:136
  547.3 40.2 %psum.69 = f32[]{:T(128)} all-reduce(f32[]{:T(128)} %get-tuple-element.396), channel_id=1, replica_groups=mesh['tile'=8,'dir'=4] {'tile','dir'}, use_global_device_ids=true, to_apply=%region_16.18 | all-reduce | flops 1 | bytes 8 | tf_op jit(solution)/shard_map/psum | solution.py:126
  591.0 4.5 collective-permute-start.25
  596.9 3.9 collective-permute-start.26
  602.3 3.9 collective-permute-done.27
  615.1 4.5 collective-permute-start.29
  642.7 38.8 %all-reduce = (f32[]{:T(128)}, f32[6]{0:T(128)S(1)}) all-reduce(f32[]{:T(128)} %fusion.224, f32[6]{0:T(128)S(1)} %convolution_bitcast_fusion), channel_id=1, replica_groups=mesh['tile'=8,'dir'=4] {'tile','dir'}, use_global_device_ids=true, to_apply=%region_18.20 | all-reduce | flops 7 | bytes 56 | tf_op jit(solution)/shard_map/psum | solution.py:136
  686.1 4.5 collective-permute-start.33
  696.9 4.2 collective-permute-done.35
  705.0 14.3 %all_gather.3 = bf16[64,2048]{1,0:T(8,128)(2,1)S(1)} all-gather(bf16[64,512]{1,0:T(8,128)(2,1)S(1)} %bitcast.390), channel_id=1, replica_groups=mesh['tile'=8,'dir'=4] {'dir'}, dimensions={1}, use_global_device_ids=true | all-gather | bytes 327680 | tf_op jit(solution)/shard_map/all_gather | solution.py:150
  (416 shorter events, 204.7 us)
Async XLA Ops:
  7.2 272.9 %reduce-scatter.2.cloned.1.call-start = ((), (), s32[]{:S(2)}) async-start(), calls=%async_computation.1 | async-start | bytes 327680 | tf_op jit(solution)/shard_map/reduce_scatter | solution.py:90
  7.2 61.8 %collective-permute-start = (bf16[6,64,2048]{2,1,0:T(8,128)(2,1)}, bf16[6,64,2048]{2,1,0:T(8,128)(2,1)}, u32[]{:S(2)}, u32[]{:S(2)}) collective-permute-start(bf16[6,64,2048]{2,1,0:T(8,128)(2,1)} %param.73), channel_id=1, source_target_pairs={{0,8},{4,12},{8,16},{12,20},{16,24},{20,28},{24,0},{28,4},{1,9},{5... | collective-permute-start | bytes 4718600 | tf_op jit(solution)/shard_map/ppermute | solution.py:17
  8.8 68.4 %collective-permute-start.1 = (bf16[6,64,2048]{2,1,0:T(8,128)(2,1)}, bf16[6,64,2048]{2,1,0:T(8,128)(2,1)}, u32[]{:S(2)}, u32[]{:S(2)}) collective-permute-start(bf16[6,64,2048]{2,1,0:T(8,128)(2,1)} %param.73), channel_id=1, source_target_pairs={{0,4},{4,8},{8,12},{12,16},{16,20},{20,24},{24,28},{28,0},{1,5},{5... | collective-permute-start | bytes 4718600 | tf_op jit(solution)/shard_map/ppermute | solution.py:17
  8.8 70.1 %collective-permute-start.2 = (bf16[6,64,2048]{2,1,0:T(8,128)(2,1)}, bf16[6,64,2048]{2,1,0:T(8,128)(2,1)}, u32[]{:S(2)}, u32[]{:S(2)}) collective-permute-start(bf16[6,64,2048]{2,1,0:T(8,128)(2,1)} %param.73), channel_id=1, source_target_pairs={{0,28},{4,0},{8,4},{12,8},{16,12},{20,16},{24,20},{28,24},{1,29},{... | collective-permute-start | bytes 4718600 | tf_op jit(solution)/shard_map/ppermute | solution.py:17
  11.4 99.4 %collective-permute-start.3 = (bf16[6,64,2048]{2,1,0:T(8,128)(2,1)}, bf16[6,64,2048]{2,1,0:T(8,128)(2,1)S(1)}, u32[]{:S(2)}, u32[]{:S(2)}) collective-permute-start(bf16[6,64,2048]{2,1,0:T(8,128)(2,1)} %param.73), channel_id=1, source_target_pairs={{0,24},{4,28},{8,0},{12,4},{16,8},{20,12},{24,16},{28,20},{1,25},{... | collective-permute-start | bytes 4718600 | tf_op jit(solution)/shard_map/ppermute | solution.py:17
  284.2 6.6 collective-permute-start.4
  286.2 5.8 collective-permute-start.5
  293.4 5.5 collective-permute-start.7
  312.1 6.7 collective-permute-start.8
  314.0 5.8 collective-permute-start.9
  323.6 5.5 collective-permute-start.11
  336.1 6.6 collective-permute-start.12
  338.0 5.8 collective-permute-start.13
  451.6 6.7 collective-permute-start.16
  453.5 5.8 collective-permute-start.17
  473.8 6.6 collective-permute-start.20
  475.7 5.8 collective-permute-start.21
  484.2 5.5 collective-permute-start.23
  589.0 6.7 collective-permute-start.24
  591.0 5.8 collective-permute-start.25
  613.2 6.6 collective-permute-start.28
  615.1 5.8 collective-permute-start.29
  684.1 6.5 collective-permute-start.32
  686.1 5.8 collective-permute-start.33
  (59 other events, 727.6 us)
Sparse Core Ops, SparseCore 0:
  259.0 21.1 reduce-scatter.1
where the time goes:
time: 734 us; the launch traced here: 728 us
  blocking collectives  215 us (29%)
  other arithmetic  123 us (17%)
  between operations  96.2 us (13%)
  waiting for transfers between devices  94.2 us (13%)
  starting transfers between devices  89 us (12%)
  local copies, waits for them, and re-layouts  84.2 us (11%)
  matrix products  25.9 us (4%)
    psum x3, blocking collectives, on_device(): lax.psum((local_totals, jnp.sum(direction * local_part)), ('tile', 'dir'))  118 us
    convert_element_type x1, other arithmetic, on_device(): summed.astype(jnp.bfloat16)  96.7 us
    psum x2, blocking collectives, global_norm(): return lax.psum(jnp.sum(residual * residual), ('tile', 'dir'))  82.5 us
    ppermute x16, starting transfers between devices, padded_2(): after = lax.ppermute(first, axis, down)  46.9 us
    ppermute x16, waiting for transfers between devices, padded_2(): after = lax.ppermute(first, axis, down)  39.4 us
    slice x52, local copies, waits for them, and re-layouts, trace_rows(): beside = jnp.roll(window, -1, axis=1)  37.7 us
    ppermute x16, starting transfers between devices, padded_2(): before = lax.ppermute(last, axis, up)  37.3 us
    ppermute x4, waiting for transfers between devices, passed_along(): lax.ppermute(array, axis, [(i, (i + by) % size) for i in range(size)])  37 us
  transfers between devices with their start and end apart: 37, of which 19 were waited for; matrix products, arithmetic and copies ran while one was open for 3% of the time, Pallas kernels for 0%

commit v1 on v0

--- a/solution.py
+++ b/solution.py
@@ -10,6 +10,10 @@
 ridge_weight = 1.0
 piston_weight = 0.002
 highest = lax.Precision.HIGHEST
+
+
+def settle_racks(sheet):
+    return lax.psum(lax.psum(sheet, axis_name="dir"), "tile")
 
 
 def passed_along(array, axis, by):
@@ -133,9 +137,7 @@
     for step_index in range(ITERS):
         local_part = active * spread(weights * surface(direction)) + ridge_weight * direction
         local_totals = jnp.dot(direction.reshape(-1), petals, precision=highest)
-        petal_totals, partial_dot = lax.psum(
-            (local_totals, jnp.sum(direction * local_part)), ("tile", "dir")
-        )
+        petal_totals, partial_dot = settle_racks((local_totals, jnp.sum(direction * local_part)))
         applied = local_part + piston_weight * jnp.dot(
             petals, petal_totals, precision=highest
         ).reshape(direction.shape)

time: 734 us -> 718 us (0.978)
  blocking collectives: 215 us -> 201 us
    psum x3 -> x6, blocking collectives: 118 us -> 66.1 us  [settle_racks(): return lax.psum(lax.psum(sheet, axis_name='dir'), 'tile')]
    psum x2 -> x3, blocking collectives: 82.5 us -> 121 us  [global_norm(): return lax.psum(jnp.sum(residual * residual), ('tile', 'dir'))]
where the time goes in v1:
time: 718 us; the launch traced here: 711 us
  blocking collectives  201 us (28%)
  other arithmetic  122 us (17%)
  between operations  96.4 us (13%)
  waiting for transfers between devices  94.2 us (13%)
  starting transfers between devices  88.4 us (12%)
  local copies, waits for them, and re-layouts  83.6 us (12%)
  matrix products  25.9 us (4%)
    psum x3, blocking collectives, global_norm(): return lax.psum(jnp.sum(residual * residual), ('tile', 'dir'))  121 us
    convert_element_type x1, other arithmetic, on_device(): summed.astype(jnp.bfloat16)  96 us
    psum x6, blocking collectives, settle_racks(): return lax.psum(lax.psum(sheet, axis_name='dir'), 'tile')  66.1 us
    ppermute x16, starting transfers between devices, padded_2(): after = lax.ppermute(first, axis, down)  46.9 us
    ppermute x16, waiting for transfers between devices, padded_2(): after = lax.ppermute(first, axis, down)  39.9 us
    slice x52, local copies, waits for them, and re-layouts, trace_rows(): beside = jnp.roll(window, -1, axis=1)  37.6 us
    ppermute x16, starting transfers between devices, padded_2(): before = lax.ppermute(last, axis, up)  36.7 us
    ppermute x4, waiting for transfers between devices, passed_along(): lax.ppermute(array, axis, [(i, (i + by) % size) for i in range(size)])  36.5 us
  transfers between devices with their start and end apart: 37, of which 19 were waited for; matrix products, arithmetic and copies ran while one was open for 3% of the time, Pallas kernels for 0%

profile of v1, /device:TPU:4, one launch (start us, length us, event | category | flops | bytes accessed | tf_op | source)
XLA Modules:
  0.0 711.0 jit_solution(13655085049809590970)
XLA Ops:
  71.1 6.1 collective-permute-done.1
  80.4 30.4 %collective-permute-done.3 = bf16[6,64,2048]{2,1,0:T(8,128)(2,1)S(1)} collective-permute-done((bf16[6,64,2048]{2,1,0:T(8,128)(2,1)}, bf16[6,64,2048]{2,1,0:T(8,128)(2,1)S(1)}, u32[]{:S(2)}, u32[]{:S(2)}) %collective-permute-start.3) | collective-permute-done | bytes 1572896 | tf_op jit(solution)/shard_map/ppermute | solution.py:21
  162.0 96.0 %add_convert_fusion = (bf16[64,2048]{1,0:T(8,128)(2,1)}, f32[64,2048]{1,0:T(8,128)}, f32[64,2048]{1,0:T(8,128)}, f32[64,2048]{1,0:T(8,128)}, f32[64,2048]{1,0:T(8,128)}) fusion(f32[65,1]{1,0:T(8,128)} %slice.2466, f32[65,2047]{1,0:T(8,128)} %slice.2465, f32[]{:T(128)} %bitcast.97, f32[65,2048]{1,0:T(8,128)} %copy-done.28, f32[]{:T(128)} %bitcast.96, ...), kind=kLoop, calls=%fused_computation.395 | loop fusion | flops 31457280 | bytes 40305024 | tf_op jit(solution)/shard_map/convert_element_type | solution.py:95
  261.6 17.6 %reduce-scatter.2.cloned.1.call-done = bf16[64,512]{1,0:T(8,128)(2,1)} async-done(((bf16[64,2048]{1,0:T(8,128)(2,1)}), bf16[64,512]{1,0:T(8,128)(2,1)}) %reduce-scatter.2.cloned.1.call-update) | async-done | bytes 65552 | tf_op jit(solution)/shard_map/reduce_scatter | solution.py:94
  285.3 4.5 collective-permute-start.5
  312.9 4.5 collective-permute-start.9
  323.8 4.2 collective-permute-done.11
  336.9 4.5 collective-permute-start.13
  364.2 9.0 %all-reduce.5 = (f32[6]{0:T(128)S(1)}, f32[]{:T(128)}) all-reduce(f32[6]{0:T(128)S(1)} %convolution_bitcast_fusion.4, f32[]{:T(128)} %get-tuple-element.387), channel_id=1, replica_groups=mesh['tile'=8,'dir'=4] {'dir'}, use_global_device_ids=true, to_apply=%region_8.10 | all-reduce | flops 7 | bytes 56 | tf_op jit(solution)/shard_map/psum | solution.py:16
  373.2 12.4 %all-reduce.2 = (f32[6]{0:T(128)S(1)}, f32[]{:T(128)}) all-reduce(f32[6]{0:T(128)S(1)} %get-tuple-element.399, f32[]{:T(128)} %get-tuple-element.400), channel_id=1, replica_groups=mesh['tile'=8,'dir'=4] {'tile'}, use_global_device_ids=true, to_apply=%region_9.11 | all-reduce | flops 7 | bytes 56 | tf_op jit(solution)/shard_map/psum | solution.py:16
  386.4 40.6 %psum.105 = f32[]{:T(128)} all-reduce(f32[]{:T(128)} %get-tuple-element.388), channel_id=1, replica_groups=mesh['tile'=8,'dir'=4] {'tile','dir'}, use_global_device_ids=true, to_apply=%region_4.6 | all-reduce | flops 1 | bytes 8 | tf_op jit(solution)/shard_map/psum | solution.py:130
  429.7 40.4 %psum.110 = f32[]{:T(128)} all-reduce(f32[]{:T(128)} %get-tuple-element.403), channel_id=1, replica_groups=mesh['tile'=8,'dir'=4] {'tile','dir'}, use_global_device_ids=true, to_apply=%region_12.14 | all-reduce | flops 1 | bytes 8 | tf_op jit(solution)/shard_map/psum | solution.py:130
  473.5 4.5 collective-permute-start.17
  484.6 4.2 collective-permute-done.19
  497.7 4.5 collective-permute-start.21
  524.9 9.5 %all-reduce.4 = (f32[6]{0:T(128)S(1)}, f32[]{:T(128)}) all-reduce(f32[6]{0:T(128)S(1)} %convolution_bitcast_fusion.2, f32[]{:T(128)} %multiply_reduce_fusion.1), channel_id=1, replica_groups=mesh['tile'=8,'dir'=4] {'dir'}, use_global_device_ids=true, to_apply=%region_16.18 | all-reduce | flops 7 | bytes 56 | tf_op jit(solution)/shard_map/psum | solution.py:16
  534.5 12.4 %all-reduce.1 = (f32[6]{0:T(128)S(1)}, f32[]{:T(128)}) all-reduce(f32[6]{0:T(128)S(1)} %get-tuple-element.397, f32[]{:T(128)} %get-tuple-element.398), channel_id=1, replica_groups=mesh['tile'=8,'dir'=4] {'tile'}, use_global_device_ids=true, to_apply=%region_17.19 | all-reduce | flops 7 | bytes 56 | tf_op jit(solution)/shard_map/psum | solution.py:16
  550.4 39.8 %psum.115 = f32[]{:T(128)} all-reduce(f32[]{:T(128)} %get-tuple-element.401), channel_id=1, replica_groups=mesh['tile'=8,'dir'=4] {'tile','dir'}, use_global_device_ids=true, to_apply=%region_20.22 | all-reduce | flops 1 | bytes 8 | tf_op jit(solution)/shard_map/psum | solution.py:130
  593.6 4.5 collective-permute-start.25
  616.4 4.5 collective-permute-start.29
  643.8 10.3 %all-reduce.3 = (f32[]{:T(128)}, f32[6]{0:T(128)S(1)}) all-reduce(f32[]{:T(128)} %fusion.224, f32[6]{0:T(128)S(1)} %convolution_bitcast_fusion), channel_id=1, replica_groups=mesh['tile'=8,'dir'=4] {'dir'}, use_global_device_ids=true, to_apply=%region_22.24 | all-reduce | flops 7 | bytes 56 | tf_op jit(solution)/shard_map/psum | solution.py:16
  654.1 12.4 %all-reduce = (f32[]{:T(128)}, f32[6]{0:T(128)S(1)}) all-reduce(f32[]{:T(128)} %get-tuple-element.395, f32[6]{0:T(128)S(1)} %get-tuple-element.396), channel_id=1, replica_groups=mesh['tile'=8,'dir'=4] {'tile'}, use_global_device_ids=true, to_apply=%region_23.25 | all-reduce | flops 7 | bytes 56 | tf_op jit(solution)/shard_map/psum | solution.py:16
  671.0 4.5 collective-permute-start.33
  688.8 13.8 %all_gather.3 = bf16[64,2048]{1,0:T(8,128)(2,1)S(1)} all-gather(bf16[64,512]{1,0:T(8,128)(2,1)S(1)} %bitcast.390), channel_id=1, replica_groups=mesh['tile'=8,'dir'=4] {'dir'}, dimensions={1}, use_global_device_ids=true | all-gather | bytes 327680 | tf_op jit(solution)/shard_map/all_gather | solution.py:152
  (420 shorter events, 219.1 us)
Async XLA Ops:
  7.2 272.0 %reduce-scatter.2.cloned.1.call-start = ((), (), s32[]{:S(2)}) async-start(), calls=%async_computation.1 | async-start | bytes 327680 | tf_op jit(solution)/shard_map/reduce_scatter | solution.py:94
  7.2 62.3 %collective-permute-start = (bf16[6,64,2048]{2,1,0:T(8,128)(2,1)}, bf16[6,64,2048]{2,1,0:T(8,128)(2,1)}, u32[]{:S(2)}, u32[]{:S(2)}) collective-permute-start(bf16[6,64,2048]{2,1,0:T(8,128)(2,1)} %param.73), channel_id=1, source_target_pairs={{0,8},{4,12},{8,16},{12,20},{16,24},{20,28},{24,0},{28,4},{1,9},{5... | collective-permute-start | bytes 4718600 | tf_op jit(solution)/shard_map/ppermute | solution.py:21
  8.8 68.4 %collective-permute-start.1 = (bf16[6,64,2048]{2,1,0:T(8,128)(2,1)}, bf16[6,64,2048]{2,1,0:T(8,128)(2,1)}, u32[]{:S(2)}, u32[]{:S(2)}) collective-permute-start(bf16[6,64,2048]{2,1,0:T(8,128)(2,1)} %param.73), channel_id=1, source_target_pairs={{0,4},{4,8},{8,12},{12,16},{16,20},{20,24},{24,28},{28,0},{1,5},{5... | collective-permute-start | bytes 4718600 | tf_op jit(solution)/shard_map/ppermute | solution.py:21
  8.8 70.1 %collective-permute-start.2 = (bf16[6,64,2048]{2,1,0:T(8,128)(2,1)}, bf16[6,64,2048]{2,1,0:T(8,128)(2,1)}, u32[]{:S(2)}, u32[]{:S(2)}) collective-permute-start(bf16[6,64,2048]{2,1,0:T(8,128)(2,1)} %param.73), channel_id=1, source_target_pairs={{0,28},{4,0},{8,4},{12,8},{16,12},{20,16},{24,20},{28,24},{1,29},{... | collective-permute-start | bytes 4718600 | tf_op jit(solution)/shard_map/ppermute | solution.py:21
  11.4 99.4 %collective-permute-start.3 = (bf16[6,64,2048]{2,1,0:T(8,128)(2,1)}, bf16[6,64,2048]{2,1,0:T(8,128)(2,1)S(1)}, u32[]{:S(2)}, u32[]{:S(2)}) collective-permute-start(bf16[6,64,2048]{2,1,0:T(8,128)(2,1)} %param.73), channel_id=1, source_target_pairs={{0,24},{4,28},{8,0},{12,4},{16,8},{20,12},{24,16},{28,20},{1,25},{... | collective-permute-start | bytes 4718600 | tf_op jit(solution)/shard_map/ppermute | solution.py:21
  283.3 6.6 collective-permute-start.4
  285.3 5.8 collective-permute-start.5
  311.0 6.7 collective-permute-start.8
  312.9 5.8 collective-permute-start.9
  322.5 5.5 collective-permute-start.11
  334.9 6.6 collective-permute-start.12
  336.9 5.8 collective-permute-start.13
  345.2 5.5 collective-permute-start.15
  471.6 6.7 collective-permute-start.16
  473.5 5.8 collective-permute-start.17
  483.3 5.5 collective-permute-start.19
  495.7 6.6 collective-permute-start.20
  497.7 5.8 collective-permute-start.21
  591.7 6.7 collective-permute-start.24
  593.6 5.8 collective-permute-start.25
  614.4 6.6 collective-permute-start.28
  616.4 5.8 collective-permute-start.29
  669.1 6.5 collective-permute-start.32
  671.0 5.8 collective-permute-start.33
  (59 other events, 722.9 us)
Sparse Core Ops, SparseCore 0:
  258.1 21.1 reduce-scatter.1
